TPU v7x, 32 devices: a whole 2x2x4 slice. The times are simulated.
32 devices in a mesh: parts: 2 (over x), wide: 16 (over z, y, core).
Axes of the slice: x: 2, y: 2, z: 4, core: 2. Of those that a mesh axis runs over, the one named last changes fastest.
Arguments:
- frames: float32 [65536, 80], P(('parts', 'wide')), parts along dimension 0, may hold values from -6 to 6
- seg_start: int32 [2048], P(('parts', 'wide')), parts along dimension 0, may hold values from 1 to 1983
- seg_dest: int32 [2048], P(('parts', 'wide')), parts along dimension 0, may hold values from -1 to 15, as said below
- rec_id: int32 [2048], P(('parts', 'wide')), parts along dimension 0, may hold values from 0 to 63
- conv_weight: float32 [240, 1024], replicated, may hold values from -0.375 to 0.375
- conv_bias: float32 [1024], replicated, may hold values from -0.5 to 0.5
- proj_weight: float32 [2048, 192], replicated, may hold values from -0.125 to 0.125
- smooth_kernel: float32 [3, 3], replicated, may hold values from 0.2 to 1
Outputs:
- smoothed: float32 [1024, 512], P(('parts', 'wide')), parts along dimension 0
There are 2 independent parts, one for each index of `parts`. A program takes and returns all parts, laid end to end along the dimension named above; an argument that names none is the same for every part. Nothing has to cross between parts.
Inputs may be any that keep to these rules, and one draw needn't show every extreme that they name: `seg_dest`: -1 marks an unused slot; on each device the used slots come first; at most 4 segments of one device go to one device, and some device reaches this; every device is assigned exactly 32 segments.
All inputs are finite; a program needn't handle non-finite values.
Results may differ from a plain program's by a relative error of at most 0.001.
Values may be sent and summed in bfloat16 or wider, within the bound.
No kernel may reach another device: no remote copies, remote signals or barrier semaphores. Data moves between devices by JAX's collectives and lax.ppermute only.
A program may use at most 64 MiB of HBM per device.

v0:
```python
import math
import jax
import jax.numpy as jnp
from jax import lax
from jax.sharding import PartitionSpec as P

FEAT = 80
CH = 1024
EMB = 192
SEGLEN = 64
SEG_DEV = 32
PRECISE = lax.Precision.HIGHEST
AFF_SCALE = 8.0


def pool_segments(windows, conv_weight, conv_bias, proj_weight):
    seg_total = windows.shape[0]
    block_size = math.gcd(seg_total, 16)
    grouped = windows.reshape(seg_total // block_size, block_size, SEGLEN + 2, FEAT)

    def one_block(win_block):
        stacked = jnp.concatenate(
            [win_block[:, 0:SEGLEN], win_block[:, 1 : SEGLEN + 1], win_block[:, 2 : SEGLEN + 2]],
            axis=2,
        )
        preact = jnp.dot(
            stacked.reshape(block_size * SEGLEN, 3 * FEAT),
            conv_weight,
            precision=PRECISE,
            preferred_element_type=jnp.float32,
        )
        activated = jax.nn.relu(preact + conv_bias).reshape(block_size, SEGLEN, CH)
        frame_mean = jnp.mean(activated, axis=1)
        deviation = activated - frame_mean[:, None, :]
        frame_std = jnp.sqrt(jnp.mean(deviation * deviation, axis=1) + 1e-05)
        return jnp.concatenate([frame_mean, frame_std], axis=1)

    pooled = lax.map(one_block, grouped).reshape(seg_total, 2 * CH)
    return jnp.dot(pooled, proj_weight, precision=PRECISE, preferred_element_type=jnp.float32)


def smooth_rows(padded_rows, smooth_kernel):
    padded = jnp.pad(padded_rows, ((0, 0), (1, 1)))
    height = padded.shape[0] - 2
    col_count = padded.shape[1] - 2
    result = jnp.zeros((height, col_count), padded.dtype)
    for row_off in range(3):
        for col_off in range(3):
            result = (
                result
                + smooth_kernel[row_off, col_off]
                * padded[row_off : row_off + height, col_off : col_off + col_count]
            )
    return result


def compact(arrived_rec):
    present = arrived_rec >= 0
    position = jnp.cumsum(present.astype(jnp.int32)) - 1
    selected = present[None, :] & (
        position[None, :] == jnp.arange(SEG_DEV, dtype=jnp.int32)[:, None]
    )
    seg_rec = jnp.sum(jnp.where(selected, arrived_rec[None, :], 0), axis=1).astype(jnp.int32)
    return (selected.astype(jnp.float32), seg_rec)


def score_panel(unit, seg_rec, panel_unit, panel_rec):
    scores = AFF_SCALE * jnp.dot(unit, panel_unit.T, preferred_element_type=jnp.float32)
    return jnp.where(seg_rec[:, None] == panel_rec[None, :], 0.0, scores)


def per_device(
    frames, seg_start, seg_dest, rec_id, conv_weight, conv_bias, proj_weight, smooth_kernel
):
    group_size = lax.axis_size("wide")
    slot_count = seg_dest.shape[0]
    pair_cap = -(-slot_count // group_size)
    matches = (seg_dest[None, :] == jnp.arange(group_size, dtype=jnp.int32)[:, None]).astype(
        jnp.int32
    )
    order_pos = jnp.sum(jnp.cumsum(matches, axis=1) * matches, axis=0) - 1
    target = jnp.where(seg_dest >= 0, seg_dest * pair_cap + order_pos, -1)
    table = target[None, :] == jnp.arange(group_size * pair_cap, dtype=jnp.int32)[:, None]
    router = table.astype(jnp.float32)
    send_rec = (jnp.sum(jnp.where(table, rec_id[None, :] + 1, 0), axis=1) - 1).reshape(
        group_size, pair_cap
    )

    def cut_one(offset):
        return lax.dynamic_slice_in_dim(frames, offset - 1, SEGLEN + 2, 0)

    windows = jax.vmap(cut_one)(seg_start)
    embedded = pool_segments(windows, conv_weight, conv_bias, proj_weight)
    outgoing = jnp.dot(router, embedded, precision=PRECISE).reshape(group_size, pair_cap, EMB)
    arrived, arrived_rec = (
        lax.all_to_all(outgoing, "wide", split_axis=0, concat_axis=0, tiled=True),
        lax.all_to_all(send_rec, "wide", split_axis=0, concat_axis=0, tiled=True),
    )
    selector, seg_rec = compact(arrived_rec.reshape(group_size * pair_cap))
    seg_rows = jnp.dot(selector, arrived.reshape(group_size * pair_cap, EMB), precision=PRECISE)
    mean_sum = lax.psum(jnp.sum(seg_rows, axis=0), "wide")
    centred = seg_rows - mean_sum / (SEG_DEV * group_size)
    unit = (centred / jnp.sqrt(jnp.sum(centred * centred, axis=1, keepdims=True) + 1e-06)).astype(
        jnp.bfloat16
    )
    total_rows = SEG_DEV * group_size
    all_rec = jnp.zeros((total_rows,), jnp.int32)
    kept_rec = all_rec
    panel_unit = lax.all_gather(unit, "wide", axis=0, tiled=True)
    panel_rec = lax.all_gather(seg_rec, "wide", axis=0, tiled=True)
    scores = score_panel(unit, seg_rec, panel_unit, panel_rec)
    affinity = scores
    kept_rec = lax.dynamic_update_slice_in_dim(kept_rec, panel_rec, jnp.int32(0), 0)
    folded = (affinity, panel_unit, kept_rec)
    affinity, all_unit, all_rec = folded
    my_index = lax.axis_index("wide")
    above = my_index * SEG_DEV - 1
    below = my_index * SEG_DEV + SEG_DEV
    above_safe = jnp.clip(above, 0, total_rows - 1)
    below_safe = jnp.clip(below, 0, total_rows - 1)
    edge_unit = jnp.concatenate(
        [
            lax.dynamic_slice_in_dim(all_unit, above_safe, 1, 0),
            lax.dynamic_slice_in_dim(all_unit, below_safe, 1, 0),
        ],
        axis=0,
    )
    edge_rec = jnp.concatenate(
        [
            lax.dynamic_slice_in_dim(all_rec, above_safe, 1, 0),
            lax.dynamic_slice_in_dim(all_rec, below_safe, 1, 0),
        ],
        axis=0,
    )
    edge_rows = score_panel(edge_unit, edge_rec, all_unit, all_rec)
    inside = jnp.stack([above >= 0, below < total_rows])
    edge_rows = jnp.where(inside[:, None], edge_rows, 0.0)
    padded = jnp.concatenate([edge_rows[0:1], affinity, edge_rows[1:2]], axis=0)
    return smooth_rows(padded, smooth_kernel)


def solution(mesh):
    in_specs = (
        P(("parts", "wide"), None),
        P(("parts", "wide")),
        P(("parts", "wide")),
        P(("parts", "wide")),
        P(),
        P(),
        P(),
        P(),
    )
    out_specs = P(("parts", "wide"), None)
    return jax.shard_map(
        per_device, mesh=mesh, in_specs=in_specs, out_specs=out_specs, check_vma=False
    )
```

profile of v0, /device:TPU:0, one launch (start us, length us, event | category | flops | bytes accessed | tf_op | source)
XLA Modules:
  0.0 302.0 jit_solution(8323069585257110534)
XLA Ops:
  3.2 7.4 %all-to-all-start = ((s32[16,1,4]{2,1,0:T(1,128)}), s32[16,1,4]{2,1,0:T(1,128)S(1)}, u32[]{:S(2)}, u32[]{:S(2)}) async-start(s32[16,1,4]{2,1,0:T(1,128)} %bitcast.7), calls=%async_computation | async-start | bytes 16384 | tf_op jit(solution)/shard_map/all_to_all | solution.py:97
  11.3 178.5 %while.12 = (s32[]{:T(128)}, f32[2048,80]{0,1:T(8,128)}, s32[64,2]{0,1:T(2,128)S(1)}, f32[64,66,80]{1,2,0:T(8,128)}, s32[]{:T(128)}) while((s32[]{:T(128)}, f32[2048,80]{0,1:T(8,128)}, s32[64,2]{0,1:T(2,128)S(1)}, f32[64,66,80]{1,2,0:T(8,128)}, s32[]{:T(128)}) %tuple.54), condition=%wide.while_cond, body=%wide.while_body.sunk | while | flops 2 | bytes 82533 | solution.py:90
  25.9 2.2 bitcast_dynamic-update-slice_fusion.2
  39.8 2.2 bitcast_dynamic-update-slice_fusion.2
  79.0 2.2 bitcast_dynamic-update-slice_fusion.2
  104.0 2.2 bitcast_dynamic-update-slice_fusion.2
  112.4 2.2 bitcast_dynamic-update-slice_fusion.2
  145.7 2.2 bitcast_dynamic-update-slice_fusion.2
  148.5 2.2 bitcast_dynamic-update-slice_fusion.2
  151.3 2.2 bitcast_dynamic-update-slice_fusion.2
  156.9 2.2 bitcast_dynamic-update-slice_fusion.2
  176.4 2.2 bitcast_dynamic-update-slice_fusion.2
  179.2 2.2 bitcast_dynamic-update-slice_fusion.2
  189.8 3.3 %copy.18 = f32[4,16,66,80]{3,2,1,0:T(8,128)} copy(f32[4,16,66,80]{2,3,1,0:T(8,128)} %bitcast.62) | data formatting | bytes 2703360 | tf_op jit(solution)/shard_map/while | solution.py:38
  193.1 26.8 %while.11 = (s32[]{:T(128)}, f32[4,16,2048]{2,1,0:T(8,128)S(1)}, f32[4,16,66,80]{3,2,1,0:T(8,128)}, f32[240,1024]{1,0:T(8,128)S(1)}, f32[1024]{0:T(1024)S(1)}, /*index=5*/s32[]{:T(128)}) while((s32[]{:T(128)}, f32[4,16,2048]{2,1,0:T(8,128)S(1)}, f32[4,16,66,80]{3,2,1,0:T(8,128)}, f32[240,1024]{1,0:T(8,128)S(1)}, f32[1024]{0:T(1024)S(1)}, ...), condition=%wide.region_8.9_spmd, body=%wide.region_5.8_spmd.sunk | while | flops 3028828160 | bytes 15691861 | solution.py:38
  194.9 4.0 %bitcast_reduce_fusion.2 = (f32[16,1024]{1,0:T(8,128)S(1)}, f32[1024,1024]{1,0:T(8,128)S(1)}) fusion(f32[1024]{0:T(1024)S(1)} %get-tuple-element.202, f32[1024,240]{1,0:T(8,128)S(1)} %bitcast.61, f32[240,1024]{1,0:T(8,128)S(1)} %get-tuple-element.201), kind=kOutput, calls=%fused_computation.1.clone.1 | convolution fusion | flops 3023028224 | bytes 6230016 | tf_op jit(solution)/shard_map/while/body/eval_jaxpr/dot_general | solution.py:26
  201.6 4.0 %bitcast_reduce_fusion.2 = (f32[16,1024]{1,0:T(8,128)S(1)}, f32[1024,1024]{1,0:T(8,128)S(1)}) fusion(f32[1024]{0:T(1024)S(1)} %get-tuple-element.202, f32[1024,240]{1,0:T(8,128)S(1)} %bitcast.61, f32[240,1024]{1,0:T(8,128)S(1)} %get-tuple-element.201), kind=kOutput, calls=%fused_computation.1.clone.1 | convolution fusion | flops 3023028224 | bytes 6230016 | tf_op jit(solution)/shard_map/while/body/eval_jaxpr/dot_general | solution.py:26
  208.3 4.0 %bitcast_reduce_fusion.2 = (f32[16,1024]{1,0:T(8,128)S(1)}, f32[1024,1024]{1,0:T(8,128)S(1)}) fusion(f32[1024]{0:T(1024)S(1)} %get-tuple-element.202, f32[1024,240]{1,0:T(8,128)S(1)} %bitcast.61, f32[240,1024]{1,0:T(8,128)S(1)} %get-tuple-element.201), kind=kOutput, calls=%fused_computation.1.clone.1 | convolution fusion | flops 3023028224 | bytes 6230016 | tf_op jit(solution)/shard_map/while/body/eval_jaxpr/dot_general | solution.py:26
  215.0 4.0 %bitcast_reduce_fusion.2 = (f32[16,1024]{1,0:T(8,128)S(1)}, f32[1024,1024]{1,0:T(8,128)S(1)}) fusion(f32[1024]{0:T(1024)S(1)} %get-tuple-element.202, f32[1024,240]{1,0:T(8,128)S(1)} %bitcast.61, f32[240,1024]{1,0:T(8,128)S(1)} %get-tuple-element.201), kind=kOutput, calls=%fused_computation.1.clone.1 | convolution fusion | flops 3023028224 | bytes 6230016 | tf_op jit(solution)/shard_map/while/body/eval_jaxpr/dot_general | solution.py:26
  224.5 6.3 %all-to-all-start.1 = ((f32[16,4,192]{2,1,0:T(4,128)}), f32[16,4,192]{2,1,0:T(4,128)S(1)}, u32[]{:S(2)}, u32[]{:S(2)}) async-start(f32[16,4,192]{2,1,0:T(4,128)} %reshape.108), calls=%async_computation.1 | async-start | bytes 131072 | tf_op jit(solution)/shard_map/all_to_all | solution.py:96
  232.9 12.4 %all-reduce.2 = s32[512]{0:T(512)S(1)} all-reduce(s32[512]{0:T(512)S(1)} %dynamic-update-slice.2), channel_id=1, replica_groups=mesh['parts'=2,'wide'=16] {'wide'}, use_global_device_ids=true, to_apply=%add.2 | all-reduce | flops 512 | bytes 4096
  247.5 29.5 %psum.7 = f32[192]{0:T(256)S(1)} all-reduce(f32[192]{0:T(256)S(1)} %get-tuple-element.101), channel_id=1, replica_groups=mesh['parts'=2,'wide'=16] {'wide'}, use_global_device_ids=true, to_apply=%region_10.11 | all-reduce | flops 192 | bytes 1536 | tf_op jit(solution)/shard_map/psum | solution.py:101
  277.2 17.9 %all_gather.7 = bf16[512,192]{1,0:T(8,128)(2,1)S(1)} all-gather(bf16[32,192]{1,0:T(8,128)(2,1)S(1)} %divide_convert_fusion), channel_id=1, replica_groups=mesh['parts'=2,'wide'=16] {'wide'}, dimensions={0}, use_global_device_ids=true | all-gather | bytes 208896 | tf_op jit(solution)/shard_map/all_gather | solution.py:109
  295.7 6.3 %fusion.7 = f32[32,512]{1,0:T(8,128)} fusion(f32[34,514]{1,0:T(8,128)S(1)} %select_maximum_fusion, f32[1,512]{1,0:T(1,128)S(1)} %get-tuple-element.89, f32[32,512]{1,0:T(8,128)S(1)} %fusion.3, f32[1,512]{1,0:T(1,128)S(1)} %get-tuple-element.88, f32[]{:T(128)} %bitcast.19, f32[]{:T(128)} %bitcast.18, f32[]{:T(128)} %bitcast.17, f32[]{:T(128)} %bitcast.16, ...), kind=kLoop, calls=%fused_computation.24 | loop fusion | flops 311296 | bytes 528420 | tf_op jit(solution)/shard_map/add | solution.py:50
  (261 shorter events, 177.2 us)
Async XLA Ops:
  0.0 220.0 %copy-start = (f32[2048,192]{0,1:T(8,128)S(1)}, f32[2048,192]{0,1:T(8,128)}, u32[]{:S(2)}) copy-start(f32[2048,192]{0,1:T(8,128)} %param.16) | copy-start | bytes 4718596
  0.0 193.1 %copy-start.1 = (f32[240,1024]{1,0:T(8,128)S(1)}, f32[240,1024]{1,0:T(8,128)}, u32[]{:S(2)}) copy-start(f32[240,1024]{1,0:T(8,128)} %param.14) | copy-start | bytes 2949124
  0.0 193.1 %copy-start.2 = (f32[1024]{0:T(1024)S(1)}, f32[1024]{0:T(1024)}, u32[]{:S(2)}) copy-start(f32[1024]{0:T(1024)} %param.15) | copy-start | bytes 12292
  3.2 221.3 %all-to-all-start = ((s32[16,1,4]{2,1,0:T(1,128)}), s32[16,1,4]{2,1,0:T(1,128)S(1)}, u32[]{:S(2)}, u32[]{:S(2)}) async-start(s32[16,1,4]{2,1,0:T(1,128)} %bitcast.7), calls=%async_computation | async-start | bytes 16384 | tf_op jit(solution)/shard_map/all_to_all | solution.py:97
  193.1 29.3 %copy-start.3 = (f32[3,3]{1,0:T(4,128)S(1)}, f32[3,3]{1,0:T(4,128)}, u32[]{:S(2)}) copy-start(f32[3,3]{1,0:T(4,128)} %param.17) | copy-start | bytes 112
  193.1 30.1 %copy-start.4 = (u32[32]{0:T(128)S(1)}, u32[32]{0:T(128)}, u32[]{:S(2)}) copy-start(u32[32]{0:T(128)} %constant.91) | copy-start | bytes 388
  224.5 22.9 %all-to-all-start.1 = ((f32[16,4,192]{2,1,0:T(4,128)}), f32[16,4,192]{2,1,0:T(4,128)S(1)}, u32[]{:S(2)}, u32[]{:S(2)}) async-start(f32[16,4,192]{2,1,0:T(4,128)} %reshape.108), calls=%async_computation.1 | async-start | bytes 131072 | tf_op jit(solution)/shard_map/all_to_all | solution.py:96
where the time goes:
time: 306 us; the launch traced here: 302 us
  local copies, waits for them, and re-layouts  191 us (62%)
  blocking collectives  59.8 us (20%)
  matrix products  18.5 us (6%)
  other arithmetic  17.7 us (6%)
  starting transfers between devices  13.7 us (4%)
    gather x192, local copies, waits for them, and re-layouts  178 us
    psum x1, blocking collectives, per_device(): mean_sum = lax.psum(jnp.sum(seg_rows, axis=0), 'wide')  29.5 us
    all_gather x1, blocking collectives, per_device(): panel_unit = lax.all_gather(unit, 'wide', axis=0, tiled=True)  17.9 us
    dot_general x4, matrix products, one_block(): jnp.dot(stacked.reshape(block_size * SEGLEN, 3 * FEAT), conv_weight, prec...  16.2 us
    unnamed x1, blocking collectives  12.4 us
    all_to_all x1, starting transfers between devices, per_device(): lax.all_to_all(send_rec, 'wide', split_axis=0, concat_axis=0, tiled=True)  7.39 us
    all_to_all x1, starting transfers between devices, per_device(): lax.all_to_all(outgoing, 'wide', split_axis=0, concat_axis=0, tiled=True)  6.35 us
    add x1, other arithmetic, smooth_rows(): result + smooth_kernel[row_off, col_off] * padded[row_off:row_off + heigh...  6.29 us
  transfers between devices with their start and end apart: 2, of which 0 were waited for; matrix products, arithmetic and copies ran while one was open for 72% of the time, Pallas kernels for 0%

commit v1 on v0

--- a/solution.py
+++ b/solution.py
@@ -106,7 +106,24 @@
     total_rows = SEG_DEV * group_size
     all_rec = jnp.zeros((total_rows,), jnp.int32)
     kept_rec = all_rec
-    panel_unit = lax.all_gather(unit, "wide", axis=0, tiled=True)
+    ways, here, step = (lax.axis_size("wide"), lax.axis_index("wide"), unit.shape[0])
+    lengths = [n * ways if d == 0 else n for d, n in enumerate(unit.shape)]
+    panel_unit = lax.dynamic_update_slice_in_dim(
+        jnp.zeros(lengths, unit.dtype), unit, here * step, axis=0
+    )
+    going_up = going_down = unit
+    for far in range(1, ways // 2 + 1):
+        going_up = lax.ppermute(going_up, "wide", [(d, (d + 1) % ways) for d in range(ways)])
+        panel_unit = lax.dynamic_update_slice_in_dim(
+            panel_unit, going_up, (here - far) % ways * step, axis=0
+        )
+        if 2 * far < ways:
+            going_down = lax.ppermute(
+                going_down, "wide", [(d, (d - 1) % ways) for d in range(ways)]
+            )
+            panel_unit = lax.dynamic_update_slice_in_dim(
+                panel_unit, going_down, (here + far) % ways * step, axis=0
+            )
     panel_rec = lax.all_gather(seg_rec, "wide", axis=0, tiled=True)
     scores = score_panel(unit, seg_rec, panel_unit, panel_rec)
     affinity = scores

time: 306 us -> 338 us (1.10)
  starting transfers between devices: 13.7 us -> 44.7 us
  blocking collectives: 59.8 us -> 41.9 us
  waiting for transfers between devices: 0.01 us -> 14.5 us
  local copies, waits for them, and re-layouts: 191 us -> 196 us
    ppermute x0 -> x15, starting transfers between devices: none -> 31 us  [the longest x7 30.9 us: per_device(): lax.ppermute(going_down, 'wide', [(d, (d - 1) % ways) for d in range(ways)])]
    all_gather x1 -> x0, blocking collectives: 17.9 us -> none  [per_device(): panel_unit = lax.all_gather(unit, 'wide', axis=0, tiled=True)]
    ppermute x0 -> x15, waiting for transfers between devices: none -> 14.5 us  [the longest x8 14.3 us: per_device(): lax.ppermute(going_up, 'wide', [(d, (d + 1) % ways) for d in range(ways)])]
    gather x192, local copies, waits for them, and re-layouts: 178 us -> 183 us
  transfers between devices with their start and end apart: 2 -> 17, of which waited for: 0 -> 7; matrix products, arithmetic and copies ran while one was open for 72% -> 66% of each run, Pallas kernels for 0% -> 0%
where the time goes in v1:
time: 338 us; the launch traced here: 335 us
  local copies, waits for them, and re-layouts  196 us (58%)
  starting transfers between devices  44.7 us (13%)
  blocking collectives  41.9 us (12%)
  matrix products  18.3 us (5%)
  other arithmetic  17.7 us (5%)
  waiting for transfers between devices  14.5 us (4%)
    gather x192, local copies, waits for them, and re-layouts  183 us
    ppermute x7, starting transfers between devices, per_device(): lax.ppermute(going_down, 'wide', [(d, (d - 1) % ways) for d in range(ways)])  30.9 us
    psum x1, blocking collectives, per_device(): mean_sum = lax.psum(jnp.sum(seg_rows, axis=0), 'wide')  29.5 us
    dot_general x4, matrix products, one_block(): jnp.dot(stacked.reshape(block_size * SEGLEN, 3 * FEAT), conv_weight, prec...  16 us
    ppermute x8, waiting for transfers between devices, per_device(): lax.ppermute(going_up, 'wide', [(d, (d + 1) % ways) for d in range(ways)])  14.3 us
    unnamed x1, blocking collectives  12.4 us
    all_to_all x1, starting transfers between devices, per_device(): lax.all_to_all(send_rec, 'wide', split_axis=0, concat_axis=0, tiled=True)  7.39 us
  transfers between devices with their start and end apart: 17, of which 7 were waited for; matrix products, arithmetic and copies ran while one was open for 66% of the time, Pallas kernels for 0%

profile of v1, /device:TPU:0, one launch (start us, length us, event | category | flops | bytes accessed | tf_op | source)
XLA Modules:
  0.0 334.6 jit_solution(13710289483722801164)
XLA Ops:
  3.2 7.4 %all-to-all-start = ((s32[16,1,4]{2,1,0:T(1,128)}), s32[16,1,4]{2,1,0:T(1,128)S(1)}, u32[]{:S(2)}, u32[]{:S(2)}) async-start(s32[16,1,4]{2,1,0:T(1,128)} %bitcast.7), calls=%async_computation | async-start | bytes 16384 | tf_op jit(solution)/shard_map/all_to_all | solution.py:97
  11.6 183.4 %while.12 = (s32[]{:T(128)}, f32[2048,80]{0,1:T(8,128)}, s32[64,2]{0,1:T(2,128)S(1)}, f32[64,66,80]{1,2,0:T(8,128)}, s32[]{:T(128)}) while((s32[]{:T(128)}, f32[2048,80]{0,1:T(8,128)}, s32[64,2]{0,1:T(2,128)S(1)}, f32[64,66,80]{1,2,0:T(8,128)}, s32[]{:T(128)}) %tuple.55), condition=%wide.while_cond, body=%wide.while_body.sunk | while | flops 2 | bytes 83033 | solution.py:90
  40.9 2.2 bitcast_dynamic-update-slice_fusion.2
  152.5 2.2 bitcast_dynamic-update-slice_fusion.2
  161.1 2.2 bitcast_dynamic-update-slice_fusion.2
  181.2 2.2 bitcast_dynamic-update-slice_fusion.2
  195.0 3.3 copy.18
  198.3 26.7 %while.11 = (s32[]{:T(128)}, f32[4,16,2048]{2,1,0:T(8,128)S(1)}, f32[4,16,66,80]{3,2,1,0:T(8,128)}, f32[240,1024]{1,0:T(8,128)S(1)}, f32[1024]{0:T(1024)S(1)}, /*index=5*/s32[]{:T(128)}) while((s32[]{:T(128)}, f32[4,16,2048]{2,1,0:T(8,128)S(1)}, f32[4,16,66,80]{3,2,1,0:T(8,128)}, f32[240,1024]{1,0:T(8,128)S(1)}, f32[1024]{0:T(1024)S(1)}, ...), condition=%wide.region_8.9_spmd, body=%wide.region_5.8_spmd.sunk | while | flops 3028828160 | bytes 15691853 | solution.py:38
  200.0 4.0 %bitcast_reduce_fusion.2 = (f32[16,1024]{1,0:T(8,128)S(1)}, f32[1024,1024]{1,0:T(8,128)S(1)}) fusion(f32[1024]{0:T(1024)S(1)} %get-tuple-element.204, f32[1024,240]{1,0:T(8,128)S(1)} %bitcast.61, f32[240,1024]{1,0:T(8,128)S(1)} %get-tuple-element.203), kind=kOutput, calls=%fused_computation.1.clone.1 | convolution fusion | flops 3023028224 | bytes 6230016 | tf_op jit(solution)/shard_map/while/body/eval_jaxpr/dot_general | solution.py:26
  206.7 4.0 %bitcast_reduce_fusion.2 = (f32[16,1024]{1,0:T(8,128)S(1)}, f32[1024,1024]{1,0:T(8,128)S(1)}) fusion(f32[1024]{0:T(1024)S(1)} %get-tuple-element.204, f32[1024,240]{1,0:T(8,128)S(1)} %bitcast.61, f32[240,1024]{1,0:T(8,128)S(1)} %get-tuple-element.203), kind=kOutput, calls=%fused_computation.1.clone.1 | convolution fusion | flops 3023028224 | bytes 6230016 | tf_op jit(solution)/shard_map/while/body/eval_jaxpr/dot_general | solution.py:26
  213.4 4.0 %bitcast_reduce_fusion.2 = (f32[16,1024]{1,0:T(8,128)S(1)}, f32[1024,1024]{1,0:T(8,128)S(1)}) fusion(f32[1024]{0:T(1024)S(1)} %get-tuple-element.204, f32[1024,240]{1,0:T(8,128)S(1)} %bitcast.61, f32[240,1024]{1,0:T(8,128)S(1)} %get-tuple-element.203), kind=kOutput, calls=%fused_computation.1.clone.1 | convolution fusion | flops 3023028224 | bytes 6230016 | tf_op jit(solution)/shard_map/while/body/eval_jaxpr/dot_general | solution.py:26
  220.1 4.0 %bitcast_reduce_fusion.2 = (f32[16,1024]{1,0:T(8,128)S(1)}, f32[1024,1024]{1,0:T(8,128)S(1)}) fusion(f32[1024]{0:T(1024)S(1)} %get-tuple-element.204, f32[1024,240]{1,0:T(8,128)S(1)} %bitcast.61, f32[240,1024]{1,0:T(8,128)S(1)} %get-tuple-element.203), kind=kOutput, calls=%fused_computation.1.clone.1 | convolution fusion | flops 3023028224 | bytes 6230016 | tf_op jit(solution)/shard_map/while/body/eval_jaxpr/dot_general | solution.py:26
  229.5 6.3 %all-to-all-start.1 = ((f32[16,4,192]{2,1,0:T(4,128)}), f32[16,4,192]{2,1,0:T(4,128)S(1)}, u32[]{:S(2)}, u32[]{:S(2)}) async-start(f32[16,4,192]{2,1,0:T(4,128)} %reshape.108), calls=%async_computation.1 | async-start | bytes 131072 | tf_op jit(solution)/shard_map/all_to_all | solution.py:96
  237.9 12.4 %all-reduce.2 = s32[512]{0:T(512)S(1)} all-reduce(s32[512]{0:T(512)S(1)} %dynamic-update-slice.2), channel_id=1, replica_groups=mesh['parts'=2,'wide'=16] {'wide'}, use_global_device_ids=true, to_apply=%add.2 | all-reduce | flops 512 | bytes 4096
  251.2 29.5 %psum.7 = f32[192]{0:T(256)S(1)} all-reduce(f32[192]{0:T(256)S(1)} %get-tuple-element.103), channel_id=1, replica_groups=mesh['parts'=2,'wide'=16] {'wide'}, use_global_device_ids=true, to_apply=%region_10.11 | all-reduce | flops 192 | bytes 1536 | tf_op jit(solution)/shard_map/psum | solution.py:101
  280.9 4.4 %collective-permute-start.1 = (bf16[32,192]{1,0:T(8,128)(2,1)S(1)}, bf16[32,192]{1,0:T(8,128)(2,1)S(1)}, u32[]{:S(2)}, u32[]{:S(2)}) collective-permute-start(bf16[32,192]{1,0:T(8,128)(2,1)S(1)} %get-tuple-element.82), channel_id=1, source_target_pairs={{0,15},{1,0},{2,1},{3,2},{4,3},{5,4},{6,5},{7,6},{8,7},{9,8},{10,9... | collective-permute-start | bytes 36872 | tf_op jit(solution)/shard_map/ppermute | solution.py:121
  286.8 4.4 %collective-permute-start.3 = (bf16[32,192]{1,0:T(8,128)(2,1)S(1)}, bf16[32,192]{1,0:T(8,128)(2,1)S(1)}, u32[]{:S(2)}, u32[]{:S(2)}) collective-permute-start(bf16[32,192]{1,0:T(8,128)(2,1)S(1)} %collective-permute-done.1), channel_id=1, source_target_pairs={{0,15},{1,0},{2,1},{3,2},{4,3},{5,4},{6,5},{7,6},{8,7},{9,8},{10,9... | collective-permute-start | bytes 36872 | tf_op jit(solution)/shard_map/ppermute | solution.py:121
  292.7 4.4 %collective-permute-start.5 = (bf16[32,192]{1,0:T(8,128)(2,1)S(1)}, bf16[32,192]{1,0:T(8,128)(2,1)S(1)}, u32[]{:S(2)}, u32[]{:S(2)}) collective-permute-start(bf16[32,192]{1,0:T(8,128)(2,1)S(1)} %collective-permute-done.3), channel_id=1, source_target_pairs={{0,15},{1,0},{2,1},{3,2},{4,3},{5,4},{6,5},{7,6},{8,7},{9,8},{10,9... | collective-permute-start | bytes 36872 | tf_op jit(solution)/shard_map/ppermute | solution.py:121
  298.5 4.4 %collective-permute-start.7 = (bf16[32,192]{1,0:T(8,128)(2,1)S(1)}, bf16[32,192]{1,0:T(8,128)(2,1)S(1)}, u32[]{:S(2)}, u32[]{:S(2)}) collective-permute-start(bf16[32,192]{1,0:T(8,128)(2,1)S(1)} %collective-permute-done.5), channel_id=1, source_target_pairs={{0,15},{1,0},{2,1},{3,2},{4,3},{5,4},{6,5},{7,6},{8,7},{9,8},{10,9... | collective-permute-start | bytes 36872 | tf_op jit(solution)/shard_map/ppermute | solution.py:121
  304.4 4.4 %collective-permute-start.9 = (bf16[32,192]{1,0:T(8,128)(2,1)S(1)}, bf16[32,192]{1,0:T(8,128)(2,1)S(1)}, u32[]{:S(2)}, u32[]{:S(2)}) collective-permute-start(bf16[32,192]{1,0:T(8,128)(2,1)S(1)} %collective-permute-done.7), channel_id=1, source_target_pairs={{0,15},{1,0},{2,1},{3,2},{4,3},{5,4},{6,5},{7,6},{8,7},{9,8},{10,9... | collective-permute-start | bytes 36872 | tf_op jit(solution)/shard_map/ppermute | solution.py:121
  310.3 4.4 %collective-permute-start.11 = (bf16[32,192]{1,0:T(8,128)(2,1)S(1)}, bf16[32,192]{1,0:T(8,128)(2,1)S(1)}, u32[]{:S(2)}, u32[]{:S(2)}) collective-permute-start(bf16[32,192]{1,0:T(8,128)(2,1)S(1)} %collective-permute-done.9), channel_id=1, source_target_pairs={{0,15},{1,0},{2,1},{3,2},{4,3},{5,4},{6,5},{7,6},{8,7},{9,8},{10,9... | collective-permute-start | bytes 36872 | tf_op jit(solution)/shard_map/ppermute | solution.py:121
  316.1 4.4 %collective-permute-start.13 = (bf16[32,192]{1,0:T(8,128)(2,1)S(1)}, bf16[32,192]{1,0:T(8,128)(2,1)S(1)}, u32[]{:S(2)}, u32[]{:S(2)}) collective-permute-start(bf16[32,192]{1,0:T(8,128)(2,1)S(1)} %collective-permute-done.11), channel_id=1, source_target_pairs={{0,15},{1,0},{2,1},{3,2},{4,3},{5,4},{6,5},{7,6},{8,7},{9,8},{10,9... | collective-permute-start | bytes 36872 | tf_op jit(solution)/shard_map/ppermute | solution.py:121
  322.0 5.8 %collective-permute-done.14 = bf16[32,192]{1,0:T(8,128)(2,1)S(1)} collective-permute-done((bf16[32,192]{1,0:T(8,128)(2,1)S(1)}, bf16[32,192]{1,0:T(8,128)(2,1)S(1)}, u32[]{:S(2)}, u32[]{:S(2)}) %collective-permute-start.14) | collective-permute-done | bytes 12320 | tf_op jit(solution)/shard_map/ppermute | solution.py:116
  328.3 6.3 %fusion.7 = f32[32,512]{1,0:T(8,128)} fusion(f32[34,514]{1,0:T(8,128)S(1)} %select_maximum_fusion, f32[1,512]{1,0:T(1,128)S(1)} %get-tuple-element.91, f32[32,512]{1,0:T(8,128)S(1)} %fusion.3, f32[1,512]{1,0:T(1,128)S(1)} %get-tuple-element.90, f32[]{:T(128)} %bitcast.19, f32[]{:T(128)} %bitcast.18, f32[]{:T(128)} %bitcast.17, f32[]{:T(128)} %bitcast.16, ...), kind=kLoop, calls=%fused_computation.24 | loop fusion | flops 311296 | bytes 528420 | tf_op jit(solution)/shard_map/add | solution.py:50
  (306 shorter events, 206.3 us)
Async XLA Ops:
  0.0 225.0 %copy-start = (f32[2048,192]{0,1:T(8,128)S(1)}, f32[2048,192]{0,1:T(8,128)}, u32[]{:S(2)}) copy-start(f32[2048,192]{0,1:T(8,128)} %param.16) | copy-start | bytes 4718596
  0.0 198.2 %copy-start.1 = (f32[240,1024]{1,0:T(8,128)S(1)}, f32[240,1024]{1,0:T(8,128)}, u32[]{:S(2)}) copy-start(f32[240,1024]{1,0:T(8,128)} %param.14) | copy-start | bytes 2949124
  0.0 198.2 %copy-start.2 = (f32[1024]{0:T(1024)S(1)}, f32[1024]{0:T(1024)}, u32[]{:S(2)}) copy-start(f32[1024]{0:T(1024)} %param.15) | copy-start | bytes 12292
  3.2 226.3 %all-to-all-start = ((s32[16,1,4]{2,1,0:T(1,128)}), s32[16,1,4]{2,1,0:T(1,128)S(1)}, u32[]{:S(2)}, u32[]{:S(2)}) async-start(s32[16,1,4]{2,1,0:T(1,128)} %bitcast.7), calls=%async_computation | async-start | bytes 16384 | tf_op jit(solution)/shard_map/all_to_all | solution.py:97
  198.2 29.3 %copy-start.3 = (f32[3,3]{1,0:T(4,128)S(1)}, f32[3,3]{1,0:T(4,128)}, u32[]{:S(2)}) copy-start(f32[3,3]{1,0:T(4,128)} %param.17) | copy-start | bytes 112
  198.2 30.0 %copy-start.4 = (u32[32]{0:T(128)S(1)}, u32[32]{0:T(128)}, u32[]{:S(2)}) copy-start(u32[32]{0:T(128)} %constant.188) | copy-start | bytes 388
  229.5 21.5 %all-to-all-start.1 = ((f32[16,4,192]{2,1,0:T(4,128)}), f32[16,4,192]{2,1,0:T(4,128)S(1)}, u32[]{:S(2)}, u32[]{:S(2)}) async-start(f32[16,4,192]{2,1,0:T(4,128)} %reshape.108), calls=%async_computation.1 | async-start | bytes 131072 | tf_op jit(solution)/shard_map/all_to_all | solution.py:96
  280.9 5.9 %collective-permute-start = (bf16[32,192]{1,0:T(8,128)(2,1)S(1)}, bf16[32,192]{1,0:T(8,128)(2,1)S(1)}, u32[]{:S(2)}, u32[]{:S(2)}) collective-permute-start(bf16[32,192]{1,0:T(8,128)(2,1)S(1)} %get-tuple-element.82), channel_id=1, source_target_pairs={{0,1},{1,2},{2,3},{3,4},{4,5},{5,6},{6,7},{7,8},{8,9},{9,10},{10,1... | collective-permute-start | bytes 36872 | tf_op jit(solution)/shard_map/ppermute | solution.py:116
  280.9 5.9 %collective-permute-start.1 = (bf16[32,192]{1,0:T(8,128)(2,1)S(1)}, bf16[32,192]{1,0:T(8,128)(2,1)S(1)}, u32[]{:S(2)}, u32[]{:S(2)}) collective-permute-start(bf16[32,192]{1,0:T(8,128)(2,1)S(1)} %get-tuple-element.82), channel_id=1, source_target_pairs={{0,15},{1,0},{2,1},{3,2},{4,3},{5,4},{6,5},{7,6},{8,7},{9,8},{10,9... | collective-permute-start | bytes 36872 | tf_op jit(solution)/shard_map/ppermute | solution.py:121
  286.8 5.9 %collective-permute-start.2 = (bf16[32,192]{1,0:T(8,128)(2,1)S(1)}, bf16[32,192]{1,0:T(8,128)(2,1)S(1)}, u32[]{:S(2)}, u32[]{:S(2)}) collective-permute-start(bf16[32,192]{1,0:T(8,128)(2,1)S(1)} %collective-permute-done), channel_id=1, source_target_pairs={{0,1},{1,2},{2,3},{3,4},{4,5},{5,6},{6,7},{7,8},{8,9},{9,10},{10,1... | collective-permute-start | bytes 36872 | tf_op jit(solution)/shard_map/ppermute | solution.py:116
  286.8 5.9 %collective-permute-start.3 = (bf16[32,192]{1,0:T(8,128)(2,1)S(1)}, bf16[32,192]{1,0:T(8,128)(2,1)S(1)}, u32[]{:S(2)}, u32[]{:S(2)}) collective-permute-start(bf16[32,192]{1,0:T(8,128)(2,1)S(1)} %collective-permute-done.1), channel_id=1, source_target_pairs={{0,15},{1,0},{2,1},{3,2},{4,3},{5,4},{6,5},{7,6},{8,7},{9,8},{10,9... | collective-permute-start | bytes 36872 | tf_op jit(solution)/shard_map/ppermute | solution.py:121
  292.7 5.9 %collective-permute-start.4 = (bf16[32,192]{1,0:T(8,128)(2,1)S(1)}, bf16[32,192]{1,0:T(8,128)(2,1)S(1)}, u32[]{:S(2)}, u32[]{:S(2)}) collective-permute-start(bf16[32,192]{1,0:T(8,128)(2,1)S(1)} %collective-permute-done.2), channel_id=1, source_target_pairs={{0,1},{1,2},{2,3},{3,4},{4,5},{5,6},{6,7},{7,8},{8,9},{9,10},{10,1... | collective-permute-start | bytes 36872 | tf_op jit(solution)/shard_map/ppermute | solution.py:116
  292.7 5.9 %collective-permute-start.5 = (bf16[32,192]{1,0:T(8,128)(2,1)S(1)}, bf16[32,192]{1,0:T(8,128)(2,1)S(1)}, u32[]{:S(2)}, u32[]{:S(2)}) collective-permute-start(bf16[32,192]{1,0:T(8,128)(2,1)S(1)} %collective-permute-done.3), channel_id=1, source_target_pairs={{0,15},{1,0},{2,1},{3,2},{4,3},{5,4},{6,5},{7,6},{8,7},{9,8},{10,9... | collective-permute-start | bytes 36872 | tf_op jit(solution)/shard_map/ppermute | solution.py:121
  298.5 5.9 %collective-permute-start.6 = (bf16[32,192]{1,0:T(8,128)(2,1)S(1)}, bf16[32,192]{1,0:T(8,128)(2,1)S(1)}, u32[]{:S(2)}, u32[]{:S(2)}) collective-permute-start(bf16[32,192]{1,0:T(8,128)(2,1)S(1)} %collective-permute-done.4), channel_id=1, source_target_pairs={{0,1},{1,2},{2,3},{3,4},{4,5},{5,6},{6,7},{7,8},{8,9},{9,10},{10,1... | collective-permute-start | bytes 36872 | tf_op jit(solution)/shard_map/ppermute | solution.py:116
  298.5 5.9 %collective-permute-start.7 = (bf16[32,192]{1,0:T(8,128)(2,1)S(1)}, bf16[32,192]{1,0:T(8,128)(2,1)S(1)}, u32[]{:S(2)}, u32[]{:S(2)}) collective-permute-start(bf16[32,192]{1,0:T(8,128)(2,1)S(1)} %collective-permute-done.5), channel_id=1, source_target_pairs={{0,15},{1,0},{2,1},{3,2},{4,3},{5,4},{6,5},{7,6},{8,7},{9,8},{10,9... | collective-permute-start | bytes 36872 | tf_op jit(solution)/shard_map/ppermute | solution.py:121
  304.4 5.9 %collective-permute-start.8 = (bf16[32,192]{1,0:T(8,128)(2,1)S(1)}, bf16[32,192]{1,0:T(8,128)(2,1)S(1)}, u32[]{:S(2)}, u32[]{:S(2)}) collective-permute-start(bf16[32,192]{1,0:T(8,128)(2,1)S(1)} %collective-permute-done.6), channel_id=1, source_target_pairs={{0,1},{1,2},{2,3},{3,4},{4,5},{5,6},{6,7},{7,8},{8,9},{9,10},{10,1... | collective-permute-start | bytes 36872 | tf_op jit(solution)/shard_map/ppermute | solution.py:116
  304.4 5.9 %collective-permute-start.9 = (bf16[32,192]{1,0:T(8,128)(2,1)S(1)}, bf16[32,192]{1,0:T(8,128)(2,1)S(1)}, u32[]{:S(2)}, u32[]{:S(2)}) collective-permute-start(bf16[32,192]{1,0:T(8,128)(2,1)S(1)} %collective-permute-done.7), channel_id=1, source_target_pairs={{0,15},{1,0},{2,1},{3,2},{4,3},{5,4},{6,5},{7,6},{8,7},{9,8},{10,9... | collective-permute-start | bytes 36872 | tf_op jit(solution)/shard_map/ppermute | solution.py:121
  310.2 5.9 %collective-permute-start.10 = (bf16[32,192]{1,0:T(8,128)(2,1)S(1)}, bf16[32,192]{1,0:T(8,128)(2,1)S(1)}, u32[]{:S(2)}, u32[]{:S(2)}) collective-permute-start(bf16[32,192]{1,0:T(8,128)(2,1)S(1)} %collective-permute-done.8), channel_id=1, source_target_pairs={{0,1},{1,2},{2,3},{3,4},{4,5},{5,6},{6,7},{7,8},{8,9},{9,10},{10,1... | collective-permute-start | bytes 36872 | tf_op jit(solution)/shard_map/ppermute | solution.py:116
  310.3 5.9 %collective-permute-start.11 = (bf16[32,192]{1,0:T(8,128)(2,1)S(1)}, bf16[32,192]{1,0:T(8,128)(2,1)S(1)}, u32[]{:S(2)}, u32[]{:S(2)}) collective-permute-start(bf16[32,192]{1,0:T(8,128)(2,1)S(1)} %collective-permute-done.9), channel_id=1, source_target_pairs={{0,15},{1,0},{2,1},{3,2},{4,3},{5,4},{6,5},{7,6},{8,7},{9,8},{10,9... | collective-permute-start | bytes 36872 | tf_op jit(solution)/shard_map/ppermute | solution.py:121
  316.1 5.9 %collective-permute-start.12 = (bf16[32,192]{1,0:T(8,128)(2,1)S(1)}, bf16[32,192]{1,0:T(8,128)(2,1)S(1)}, u32[]{:S(2)}, u32[]{:S(2)}) collective-permute-start(bf16[32,192]{1,0:T(8,128)(2,1)S(1)} %collective-permute-done.10), channel_id=1, source_target_pairs={{0,1},{1,2},{2,3},{3,4},{4,5},{5,6},{6,7},{7,8},{8,9},{9,10},{10,1... | collective-permute-start | bytes 36872 | tf_op jit(solution)/shard_map/ppermute | solution.py:116
  316.1 5.9 %collective-permute-start.13 = (bf16[32,192]{1,0:T(8,128)(2,1)S(1)}, bf16[32,192]{1,0:T(8,128)(2,1)S(1)}, u32[]{:S(2)}, u32[]{:S(2)}) collective-permute-start(bf16[32,192]{1,0:T(8,128)(2,1)S(1)} %collective-permute-done.11), channel_id=1, source_target_pairs={{0,15},{1,0},{2,1},{3,2},{4,3},{5,4},{6,5},{7,6},{8,7},{9,8},{10,9... | collective-permute-start | bytes 36872 | tf_op jit(solution)/shard_map/ppermute | solution.py:121
  322.0 5.9 %collective-permute-start.14 = (bf16[32,192]{1,0:T(8,128)(2,1)S(1)}, bf16[32,192]{1,0:T(8,128)(2,1)S(1)}, u32[]{:S(2)}, u32[]{:S(2)}) collective-permute-start(bf16[32,192]{1,0:T(8,128)(2,1)S(1)} %collective-permute-done.12), channel_id=1, source_target_pairs={{0,1},{1,2},{2,3},{3,4},{4,5},{5,6},{6,7},{7,8},{8,9},{9,10},{10,1... | collective-permute-start | bytes 36872 | tf_op jit(solution)/shard_map/ppermute | solution.py:116
